TPU v7x, 256 devices: a whole 4x4x8 slice. The times are simulated.
256 devices in a mesh: req: 32 (over z, x), tp: 8 (over y, core).
Axes of the slice: x: 4, y: 4, z: 8, core: 2. Of those that a mesh axis runs over, the one named last changes fastest.
Arguments:
- hidden: bfloat16 [8192, 2048], P('req'), may hold values from -6 to 6
- kv_cache: bfloat16 [2, 1024, 128, 2048], P(None, 'req', None, 'tp'), may hold values from -64 to 64
- page_table: int32 [128, 8], P('req'), may hold values from 0 to 31, as said below
- cache_lens: int32 [128], P('req'), may hold values from 1 to 1024
- parents: int32 [128, 64], P('req'), may hold values from 0 to 62, as said below
- accepted: int32 [128, 8], P('req'), may hold values from 0 to 14, as said below
- attn_gain: float32 [2048], replicated, may hold values from 0.1 to 1.9
- w_qkv: bfloat16 [2048, 3, 2048], P(None, None, 'tp'), may hold values from -0.125 to 0.125
- qk_gain: float32 [2, 2048], P(None, 'tp'), may hold values from 0.5 to 8
- w_out: bfloat16 [2048, 2048], P('tp'), may hold values from -0.5 to 0.5
- moe_gain: float32 [2048], replicated, may hold values from 0.1 to 1.9
- routes: int32 [8192, 8], P('req'), may hold values from 0 to 63, all different within a row; in each aligned block of 256 rows (0 to 255, 256 to 511, ...) at most 40 rows name the same one
- route_weights: float32 [8192, 8], P('req'), may hold values from 0.1 to 1
- w_gate_up: bfloat16 [32, 2048, 2, 2048], P('req', None, None, 'tp'), may hold values from -0.125 to 0.125
- w_down: bfloat16 [32, 2048, 2048], P('req', 'tp'), may hold values from -0.1875 to 0.1875
Outputs:
- output: bfloat16 [8192, 2048], P('req', 'tp')
- accepted_kv: bfloat16 [2, 1024, 2048], P(None, 'req', 'tp')
Inputs may be any that keep to these rules, and one draw needn't show every extreme that they name: `page_table`: values lie in the block of 32 pages of the request's group of 4 requests; within a group every page is used once. parents[r, 0] = 0 and parents[r, j] < j for j >= 1. accepted[r] are the first 8 slots, from the root down, of a path in request r's tree. `routes`: in each aligned block of 256 rows (the tokens of one index of req), no expert is named by more than 40 rows.
All inputs are finite; a program needn't handle non-finite values.
Results may differ from a plain program's by a relative error of at most 0.012.
The roundings to bfloat16 on the way count: a program that leaves them out, or rounds other values in their place, can miss the bound.
Values may be sent and summed in bfloat16 or wider, within the bound.
No kernel may reach another device: no remote copies, remote signals or barrier semaphores. Data moves between devices by JAX's collectives and lax.ppermute only.
A program may use at most 128 MiB of HBM per device.

v0:
```python
import jax
import jax.numpy as jnp
from jax import lax
from jax.sharding import Mesh, PartitionSpec as P

HD = 128
FFE = 1024
EXPERTS = 64
CAP = 40
TP = ("th", "tl", "tc")
norm_eps = 1e-05
rope_base = 10000.0
masked_score = -1e30


def rms_scale(values, gain):
    return values * lax.rsqrt(jnp.mean(values * values, axis=-1, keepdims=True) + norm_eps) * gain


def tree_masks(parents):
    slot_count = parents.shape[-1]
    slot_ids = jnp.arange(slot_count, dtype=jnp.int32)
    parent_hot = (parents[..., :, None] == slot_ids).astype(jnp.float32)
    ancestry = jnp.minimum(jnp.eye(slot_count, dtype=jnp.float32) + parent_hot, 1.0)
    for squaring in range(slot_count.bit_length()):
        ancestry = jnp.minimum(
            jnp.einsum("rij,rjk->rik", ancestry, ancestry, precision=lax.Precision.HIGHEST), 1.0
        )
    depths = jnp.sum(ancestry, axis=-1).astype(jnp.int32) - 1
    return (ancestry, depths)


def rotate(values, positions):
    head_dim = values.shape[-1]
    half_dim = head_dim // 2
    frequency = rope_base ** (-jnp.arange(half_dim, dtype=jnp.float32) * 2.0 / head_dim)
    angles = positions.astype(jnp.float32)[:, None] * frequency[None, :]
    cosine = jnp.cos(angles)[:, None, :]
    sine_part = jnp.sin(angles)[:, None, :]
    first_half = values[..., :half_dim]
    second = values[..., half_dim:]
    return jnp.concatenate(
        [first_half * cosine - second * sine_part, second * cosine + first_half * sine_part],
        axis=-1,
    )


def local(
    hidden,
    kv_cache,
    page_table,
    cache_lens,
    parents,
    accepted,
    attn_gain,
    w_qkv,
    qk_gain,
    w_out,
    moe_gain,
    routes,
    route_weights,
    w_gate_up,
    w_down,
):
    tok_rows, model_width = hidden.shape
    th = lax.axis_index("th")
    tl = lax.axis_index("tl")
    tc = lax.axis_index("tc")
    tp_count = lax.axis_size(TP)
    req_count = lax.axis_size("req")
    slice_width = model_width // tp_count
    slice_start = ((th * lax.axis_size("tl") + tl) * lax.axis_size("tc") + tc) * slice_width
    req_local, draft_len = parents.shape
    feat_dev = w_qkv.shape[2]
    local_heads = feat_dev // HD
    ancestry, depths = tree_masks(parents)
    positions = (cache_lens[:, None] + depths).reshape(-1)
    normed_in = rms_scale(hidden.astype(jnp.float32), attn_gain).astype(jnp.bfloat16)
    projected = jnp.dot(
        normed_in, w_qkv.reshape(model_width, 3 * feat_dev), preferred_element_type=jnp.float32
    ).reshape(tok_rows, 3, feat_dev)
    query_raw = projected[:, 0]
    key_raw = projected[:, 1]
    values_new = projected[:, 2].astype(jnp.bfloat16)
    query_total, key_total = lax.psum(
        (jnp.sum(query_raw * query_raw, axis=-1), jnp.sum(key_raw * key_raw, axis=-1)), TP
    )
    query_normed = query_raw * lax.rsqrt(query_total[:, None] / model_width + norm_eps) * qk_gain[0]
    key_normed = key_raw * lax.rsqrt(key_total[:, None] / model_width + norm_eps) * qk_gain[1]
    query_rot = rotate(query_normed.reshape(tok_rows, local_heads, HD), positions).astype(
        jnp.bfloat16
    )
    keys_new = rotate(key_normed.reshape(tok_rows, local_heads, HD), positions).astype(jnp.bfloat16)
    page_rows = kv_cache[:, page_table.reshape(-1)]
    context = page_table.shape[1] * kv_cache.shape[2]
    cache_keys = page_rows[0].reshape(req_local, context, local_heads, HD)
    cache_values = page_rows[1].reshape(req_local, context, local_heads, HD)
    query_blocks = query_rot.reshape(req_local, draft_len, local_heads, HD)
    key_blocks = keys_new.reshape(req_local, draft_len, local_heads, HD)
    value_blocks = values_new.reshape(req_local, draft_len, local_heads, HD)
    score_scale = HD ** (-0.5)
    cache_scores = (
        jnp.einsum("rjhd,rchd->rhjc", query_blocks, cache_keys, preferred_element_type=jnp.float32)
        * score_scale
    )
    live_keys = jnp.arange(context, dtype=jnp.int32)[None, :] < cache_lens[:, None]
    cache_scores = jnp.where(live_keys[:, None, None, :], cache_scores, masked_score)
    draft_scores = (
        jnp.einsum("rjhd,rihd->rhji", query_blocks, key_blocks, preferred_element_type=jnp.float32)
        * score_scale
    )
    draft_scores = jnp.where(ancestry[:, None, :, :] > 0.5, draft_scores, masked_score)
    scores = jnp.concatenate([cache_scores, draft_scores], axis=-1)
    row_max = jnp.max(scores, axis=-1, keepdims=True)
    weights = jnp.exp(scores - row_max)
    probabilities = (weights / jnp.sum(weights, axis=-1, keepdims=True)).astype(jnp.bfloat16)
    all_values = jnp.concatenate([cache_values, value_blocks], axis=1)
    attn_heads = (
        jnp.einsum("rhjc,rchd->rjhd", probabilities, all_values, preferred_element_type=jnp.float32)
        .astype(jnp.bfloat16)
        .reshape(tok_rows, feat_dev)
    )
    attn_term = jnp.dot(attn_heads, w_out, preferred_element_type=jnp.float32)
    residual = hidden.astype(jnp.float32) + lax.psum(attn_term, TP)
    normed_moe = rms_scale(residual, moe_gain).astype(jnp.bfloat16)
    residual_share = lax.dynamic_slice_in_dim(residual, slice_start, slice_width, 1)
    experts_here = EXPERTS // req_count
    tok_ids = jnp.arange(tok_rows, dtype=jnp.int32)
    route_hot = (routes[:, :, None] == jnp.arange(EXPERTS, dtype=jnp.int32)).astype(jnp.float32)
    per_token = jnp.sum(route_hot, axis=1)
    weight_of = jnp.sum(route_weights[:, :, None] * route_hot, axis=1)
    earlier = (tok_ids[:, None] > tok_ids[None, :]).astype(jnp.bfloat16)
    slot_of = jnp.dot(earlier, per_token.astype(jnp.bfloat16), preferred_element_type=jnp.float32)
    capacity = CAP
    cap_ids = jnp.arange(capacity, dtype=jnp.float32)
    picked_here = lax.dynamic_index_in_dim(
        per_token.reshape(tok_rows, req_count, experts_here), th, axis=2, keepdims=False
    ).T
    slot_here = lax.dynamic_index_in_dim(
        slot_of.reshape(tok_rows, req_count, experts_here), th, axis=2, keepdims=False
    ).T
    select = jnp.where(
        (picked_here[:, None, :] > 0.5) & (slot_here[:, None, :] == cap_ids[None, :, None]),
        1.0,
        0.0,
    ).astype(jnp.bfloat16)
    half_width = model_width // 2
    normed_half = lax.dynamic_slice_in_dim(normed_moe, tc * half_width, half_width, 1)
    send_rows = jnp.einsum(
        "ict,tw->icw", select, normed_half, preferred_element_type=jnp.float32
    ).astype(jnp.bfloat16)
    received = lax.all_to_all(send_rows, "req", 0, 0, tiled=True)
    rows = lax.all_gather(received, "tc", axis=2, tiled=True)
    gate_up = jnp.einsum("scw,wgu->scgu", rows, w_gate_up[0], preferred_element_type=jnp.float32)
    activated = (jax.nn.silu(gate_up[..., 0, :]) * gate_up[..., 1, :]).astype(jnp.bfloat16)
    units_dev = w_down.shape[1]
    down = w_down[0].reshape(units_dev, 2, 2, 2, slice_width)
    partial = jnp.einsum(
        "scu,uhlkd->shckld", activated, down, preferred_element_type=jnp.float32
    ).astype(jnp.bfloat16)
    partial = partial.reshape(req_count, 2, capacity, 4 * slice_width)
    partial = lax.psum_scatter(partial, "tc", scatter_dimension=3, tiled=True)
    partial = lax.psum_scatter(partial, "tl", scatter_dimension=3, tiled=True)
    back = partial.reshape(req_count * 2, capacity, slice_width)
    returned = lax.all_to_all(back, ("req", "th"), 0, 0, tiled=True)
    combine = weight_of[:, :, None] * (slot_of[:, :, None] == cap_ids[None, None, :])
    mixture = jnp.dot(
        combine.reshape(tok_rows, EXPERTS * capacity),
        returned.reshape(EXPERTS * capacity, slice_width).astype(jnp.float32),
        precision=lax.Precision.HIGHEST,
        preferred_element_type=jnp.float32,
    )
    output = (residual_share + mixture).astype(jnp.bfloat16)
    picked_rows = (jnp.arange(req_local, dtype=jnp.int32)[:, None] * draft_len + accepted).reshape(
        -1
    )
    accepted_kv = jnp.stack(
        [keys_new.reshape(tok_rows, feat_dev)[picked_rows], values_new[picked_rows]]
    )
    return (output, accepted_kv)


def solution(mesh):
    req_count = mesh.shape["req"]
    devices = mesh.devices.reshape(req_count, 2, 2, mesh.shape["tp"] // 4)
    split_mesh = Mesh(devices, ("req",) + TP)
    return jax.shard_map(
        local,
        mesh=split_mesh,
        in_specs=(
            P("req", None),
            P(None, "req", None, TP),
            P("req", None),
            P("req"),
            P("req", None),
            P("req", None),
            P(),
            P(None, None, TP),
            P(None, TP),
            P(TP, None),
            P(),
            P("req", None),
            P("req", None),
            P("req", None, None, TP),
            P("req", TP, None),
        ),
        out_specs=(P("req", TP), P(None, "req", TP)),
        check_vma=False,
    )
```

profile of v0, /device:TPU:32, one launch (start us, length us, event | category | flops | bytes accessed | tf_op | source)
XLA Modules:
  0.0 378.7 jit_solution(12945470743647845171)
XLA Ops:
  7.3 1.6 fusion.11
  8.9 4.8 %copy.67 = bf16[2048,3,256]{0,2,1:T(8,128)(2,1)} copy(bf16[2048,3,256]{2,0,1:T(8,128)(2,1)} %param.22) | data formatting | bytes 6291456 | tf_op args[7]
  13.8 3.0 fusion.2
  16.8 0.8 copy-done.6
  18.1 0.4 convolution_minimum_fusion.6
  18.5 0.3 convolution_minimum_fusion.5
  18.8 0.3 convolution_minimum_fusion.4
  19.0 0.3 convolution_minimum_fusion.3
  19.3 0.3 convolution_minimum_fusion.2
  19.8 0.4 fusion.98
  20.3 0.6 broadcast_compare_fusion
  21.0 0.3 multiply_cosine_fusion
  21.3 14.9 %all-reduce = (f32[256]{0:T(256)S(1)}, f32[256]{0:T(256)S(1)}) all-reduce(f32[256]{0:T(256)S(1)} %get-tuple-element.3, f32[256]{0:T(256)S(1)} %get-tuple-element.2), channel_id=1, replica_groups=mesh['req'=32,'th'=2,'tl'=2,'tc'=2] {'th','tl','tc'}, use_global_device_ids=true, to_apply=%region_5.0 | all-reduce | flops 512 | bytes 4096 | tf_op jit(solution)/shard_map/psum | solution.py:85
  37.1 0.8 copy.76
  38.0 0.8 copy.77
  39.0 0.8 copy.70
  39.8 4.9 %gather_fusion = bf16[32,2,128,256]{3,2,1,0:T(8,128)(2,1)} fusion(bf16[2,32,128,256]{3,2,1,0:T(8,128)(2,1)} %param.16, s32[1024]{0:T(1024)S(1)} %pad_clamp_fusion.1), kind=kCustom, calls=%fused_computation | custom fusion | bytes 8388736 | tf_op jit(solution)/shard_map/gather | solution.py:94
  44.7 4.7 %fusion.96 = (bf16[1,32,128,256]{3,2,0,1:T(8,128)(2,1)}, bf16[1,32,128,256]{3,2,0,1:T(8,128)(2,1)}) fusion(bf16[2,32,128,256]{3,2,0,1:T(8,128)(2,1)} %bitcast.107), kind=kLoop, calls=%fused_computation.138 | loop fusion | bytes 8388608 | tf_op jit(solution)/shard_map/slice | solution.py:96
  49.4 2.5 reshape_squeeze.10
  52.0 4.0 %reshape_squeeze.9 = bf16[4,1024,2,128]{3,2,1,0:T(2,128)(2,1)} reshape(bf16[1,32,128,256]{3,2,0,1:T(8,128)(2,1)} %get-tuple-element.11) | data formatting | bytes 4194304 | tf_op jit(solution)/shard_map/reshape;squeeze | solution.py:97
  55.9 1.9 copy.69
  57.8 1.0 fusion.99
  58.9 0.4 fusion.100
  59.2 0.5 fusion.18
  59.8 0.8 fusion.48
  60.8 1.8 fusion.70
  62.6 0.7 select_reduce_fusion
  63.8 0.5 copy-done.9
  64.3 69.2 %all-reduce.3.cloned.1.call-done = f32[256,2048]{1,0:T(8,128)} async-done(((f32[256,2048]{1,0:T(8,128)}), f32[256,2048]{1,0:T(8,128)}) %all-reduce.3.cloned.1.call-update) | async-done | bytes 2097168 | tf_op jit(solution)/shard_map/psum | solution.py:124
  133.5 1.9 multiply_reduce_fusion
  135.5 1.0 convolution_convert_fusion
  136.5 70.3 %all_to_all.10 = bf16[32,40,1024]{2,1,0:T(8,128)(2,1)} all-to-all(bf16[32,40,1024]{2,1,0:T(8,128)(2,1)S(1)} %convolution_convert_fusion), channel_id=1, replica_groups=mesh['req'=32,'th'=2,'tl'=2,'tc'=2] {'req'}, dimensions={0} | all-to-all | bytes 5242880 | tf_op jit(solution)/shard_map/all_to_all | solution.py:152
  207.1 1.0 copy-done.4
  208.0 1.6 reshape_squeeze.11
  209.6 14.3 %all-gather.2.cloned.1.call-done = bf16[32,40,2048]{2,1,0:T(8,128)(2,1)} async-done(((bf16[32,40,1024]{2,1,0:T(8,128)(2,1)}), bf16[32,40,2048]{2,1,0:T(8,128)(2,1)}) %all-gather.2.cloned.1.call-update) | async-done | bytes 5242896 | tf_op jit(solution)/shard_map/all_gather | solution.py:153
  224.0 5.5 %fusion = f32[32,40,2,256]{3,1,2,0:T(8,128)S(1)} fusion(bf16[32,40,2048]{2,1,0:T(8,128)(2,1)} %all-gather.2.cloned.1.call-done, bf16[2048,2,256]{2,1,0:T(2,128)(2,1)} %bitcast.119), kind=kOutput, calls=%fused_computation.3 | convolution fusion | flops 2684354560 | bytes 9961472 | tf_op jit(solution)/shard_map/scw,wgu->scgu/dot_general | solution.py:154
  229.5 4.0 %convert_bitcast_fusion = bf16[32,2,40,2,2,256]{5,2,3,4,1,0:T(8,128)(2,1)} fusion(bf16[256,2,2,2,256]{4,3,2,1,0:T(2,128)(2,1)S(1)} %copy-done.5, f32[32,40,2,256]{3,1,2,0:T(8,128)S(1)} %fusion), kind=kOutput, calls=%fused_computation.5 | convolution fusion | flops 1346764800 | bytes 8912896 | tf_op jit(solution)/shard_map/scu,uhlkd->shckld/dot_general | solution.py:158
  233.5 10.3 %copy.81 = bf16[32,2,40,2,2,256]{5,4,3,2,1,0:T(2,128)(2,1)} copy(bf16[32,2,40,2,2,256]{5,2,3,4,1,0:T(8,128)(2,1)} %convert_bitcast_fusion) | data formatting | bytes 10485760 | tf_op jit(solution)/shard_map/convert_element_type | solution.py:160
  243.8 9.3 %reshape.284 = bf16[32,2,40,1024]{3,2,1,0:T(8,128)(2,1)} reshape(bf16[32,2,40,2,2,256]{5,4,3,2,1,0:T(2,128)(2,1)} %copy.81) | data formatting | bytes 10485760 | tf_op jit(solution)/shard_map/reshape | solution.py:161
  253.2 19.7 %reduce-scatter.3.cloned.1.call-done = bf16[32,2,40,512]{3,2,1,0:T(8,128)(2,1)} async-done(((bf16[32,2,40,1024]{3,2,1,0:T(8,128)(2,1)}), bf16[32,2,40,512]{3,2,1,0:T(8,128)(2,1)}) %reduce-scatter.3.cloned.1.call-update) | async-done | bytes 2621456 | tf_op jit(solution)/shard_map/reduce_scatter | solution.py:162
  273.0 46.4 %reduce-scatter.5.cloned.1.call-done = bf16[32,2,40,256]{3,2,1,0:T(8,128)(2,1)} async-done(((bf16[32,2,40,512]{3,2,1,0:T(8,128)(2,1)}), bf16[32,2,40,256]{3,2,1,0:T(8,128)(2,1)}) %reduce-scatter.5.cloned.1.call-update) | async-done | bytes 1310736 | tf_op jit(solution)/shard_map/reduce_scatter | solution.py:163
  319.4 12.8 %all-to-all-start.1 = ((bf16[64,40,256]{2,1,0:T(8,128)(2,1)}), bf16[64,40,256]{2,1,0:T(8,128)(2,1)}, u32[]{:S(2)}, u32[]{:S(2)}) async-start(bf16[64,40,256]{2,1,0:T(8,128)(2,1)} %bitcast.108), calls=%async_computation.3 | async-start | bytes 2621440 | tf_op jit(solution)/shard_map/all_to_all | solution.py:165
  332.2 1.0 slice_bitcast_fusion
  333.4 0.6 gather_fusion.2
  334.0 0.6 gather_fusion.1
  334.6 0.6 pad_maximum_fusion.2
  335.3 32.4 %all-to-all-done.1 = bf16[64,40,256]{2,1,0:T(8,128)(2,1)} async-done(((bf16[64,40,256]{2,1,0:T(8,128)(2,1)}), bf16[64,40,256]{2,1,0:T(8,128)(2,1)}, u32[]{:S(2)}, u32[]{:S(2)}) %all-to-all-start.1) | async-done | bytes 1310752 | tf_op jit(solution)/shard_map/all_to_all | solution.py:165
  367.7 4.4 %fusion.40 = bf16[256,256]{1,0:T(8,128)(2,1)} fusion(bf16[64,40,256]{2,1,0:T(8,128)(2,1)} %all-to-all-done.1, f32[256,64]{0,1:T(8,128)} %get-tuple-element.4, f32[256,64]{0,1:T(8,128)} %copy-done.9, f32[256,2048]{1,0:T(8,128)S(1)} %get-tuple-element.9, s32[]{:T(128)S(6)} %select_n.47), kind=kOutput, calls=%fused_computation.47 | convolution fusion | flops 2014707712 | bytes 1835012 | tf_op jit(solution)/shard_map/dot_general | solution.py:167
  (88 shorter events, 3.3 us)
Async XLA Ops:
  7.2 53.6 %copy-start = (bf16[256,2048]{1,0:T(8,128)(2,1)S(1)}, bf16[256,2048]{1,0:T(8,128)(2,1)}, u32[]{:S(2)}) copy-start(bf16[256,2048]{1,0:T(8,128)(2,1)} %param.24) | copy-start | bytes 3145732
  7.2 126.3 %all-reduce.3.cloned.1.call-start = ((), (), s32[]{:S(2)}) async-start(), calls=%async_computation.4 | async-start | bytes 4194304 | tf_op jit(solution)/shard_map/psum | solution.py:124
  8.9 4.9 %copy-start.2 = (bf16[256,2048]{1,0:T(8,128)(2,1)S(1)}, bf16[256,2048]{1,0:T(8,128)(2,1)}, u32[]{:S(2)}) copy-start(bf16[256,2048]{1,0:T(8,128)(2,1)} %param.15) | copy-start | bytes 3145732
  8.9 4.9 %copy-start.19 = (f32[2048]{0:T(1024)S(1)}, f32[2048]{0:T(1024)}, u32[]{:S(2)}) copy-start(f32[2048]{0:T(1024)} %param.21) | copy-start | bytes 24580
  13.7 4.0 %copy-start.15 = (s32[4,8]{1,0:T(4,128)S(1)}, s32[4,8]{1,0:T(4,128)}, u32[]{:S(2)}) copy-start(s32[4,8]{1,0:T(4,128)} %param.17) | copy-start | bytes 388
  13.7 4.1 %copy-start.16 = (s32[4,8]{1,0:T(4,128)S(1)}, s32[4,8]{1,0:T(4,128)}, u32[]{:S(2)}) copy-start(s32[4,8]{1,0:T(4,128)} %param.20) | copy-start | bytes 388
  13.7 4.2 %copy-start.17 = (f32[2,256]{1,0:T(2,128)S(1)}, f32[2,256]{1,0:T(2,128)}, u32[]{:S(2)}) copy-start(f32[2,256]{1,0:T(2,128)} %param.23) | copy-start | bytes 6148
  13.8 4.3 %copy-start.14 = (s32[4]{0:T(128)S(1)}, s32[4]{0:T(128)}, u32[]{:S(2)}) copy-start(s32[4]{0:T(128)} %param.18) | copy-start | bytes 52
  13.8 4.3 %copy-start.18 = (s32[4,64]{1,0:T(4,128)S(1)}, s32[4,64]{1,0:T(4,128)}, u32[]{:S(2)}) copy-start(s32[4,64]{1,0:T(4,128)} %param.19) | copy-start | bytes 3076
  16.8 0.9 copy-start.6
  57.8 1.0 copy-start.7
  57.8 1.0 copy-start.8
  57.8 1.0 copy-start.11
  58.9 0.9 copy-start.10
  60.8 1.9 copy-start.12
  60.8 1.9 copy-start.13
  62.5 71.0 %copy-start.3 = (bf16[256,2048]{1,0:T(8,128)(2,1)S(1)}, bf16[256,2048]{1,0:T(8,128)(2,1)}, u32[]{:S(2)}) copy-start(bf16[256,2048]{1,0:T(8,128)(2,1)} %param.15) | copy-start | bytes 3145732
  62.6 161.4 %all-gather.2.cloned.1.call-start = ((), (), s32[]{:S(2)}) async-start(), calls=%async_computation.5 | async-start | bytes 7864320 | tf_op jit(solution)/shard_map/all_gather | solution.py:153
  63.6 0.6 copy-start.9
  64.3 71.2 %dynamic-slice-start = ((f32[2048]{0:T(1024)}, s32[]{:T(128)}), f32[1024]{0:T(1024)S(1)}, s32[]{:S(2)}) async-start(f32[2048]{0:T(1024)} %param.25, s32[]{:T(128)} %select_n.50), calls=%async_computation.8 | async-start | bytes 8704 | tf_op jit(solution)/shard_map/dynamic_slice | solution.py:148
  206.8 1.2 copy-start.4
  206.8 66.1 %reduce-scatter.3.cloned.1.call-start = ((), (), s32[]{:S(2)}) async-start(), calls=%async_computation.6 | async-start | bytes 7864320 | tf_op jit(solution)/shard_map/reduce_scatter | solution.py:162
  224.0 5.5 %copy-start.5 = (bf16[256,2,2,2,256]{4,3,2,1,0:T(2,128)(2,1)S(1)}, bf16[256,2,2,2,256]{4,3,2,1,0:T(2,128)(2,1)}, u32[]{:S(2)}) copy-start(bf16[256,2,2,2,256]{4,3,2,1,0:T(2,128)(2,1)} %reshape_squeeze.11) | copy-start | bytes 3145732
  253.2 66.2 %reduce-scatter.5.cloned.1.call-start = ((), (), s32[]{:S(2)}) async-start(), calls=%async_computation.7 | async-start | bytes 3932160 | tf_op jit(solution)/shard_map/reduce_scatter | solution.py:163
  319.4 48.3 %all-to-all-start.1 = ((bf16[64,40,256]{2,1,0:T(8,128)(2,1)}), bf16[64,40,256]{2,1,0:T(8,128)(2,1)}, u32[]{:S(2)}, u32[]{:S(2)}) async-start(bf16[64,40,256]{2,1,0:T(8,128)(2,1)} %bitcast.108), calls=%async_computation.3 | async-start | bytes 2621440 | tf_op jit(solution)/shard_map/all_to_all | solution.py:165
  367.7 4.4 %copy-start.1 = (bf16[256,2048]{1,0:T(8,128)(2,1)S(1)}, bf16[256,2048]{1,0:T(8,128)(2,1)}, u32[]{:S(2)}) copy-start(bf16[256,2048]{1,0:T(8,128)(2,1)} %param.24) | copy-start | bytes 3145732
Sparse Core Ops, SparseCore 0:
  62.7 70.7 all-reduce.2
  206.9 16.9 all-gather.1
  253.3 19.5 reduce-scatter.2
  275.3 44.0 reduce-scatter.4
where the time goes:
time: 380 us; the launch traced here: 379 us
  waiting for transfers between devices  182 us (48%)
  blocking collectives  85.2 us (22%)
  local copies, waits for them, and re-layouts  52.8 us (14%)
  matrix products  24.1 us (6%)
  between operations  14.3 us (4%)
  starting transfers between devices  13.1 us (3%)
  other arithmetic  7 us (2%)
    all_to_all x1, blocking collectives, local(): received = lax.all_to_all(send_rows, 'req', 0, 0, tiled=True)  70.3 us
    psum x1, waiting for transfers between devices, local(): residual = hidden.astype(jnp.float32) + lax.psum(attn_term, TP)  69.2 us
    reduce_scatter x1, waiting for transfers between devices, local(): partial = lax.psum_scatter(partial, 'tl', scatter_dimension=3, tiled=True)  46.4 us
    all_to_all x1, waiting for transfers between devices, local(): returned = lax.all_to_all(back, ('req', 'th'), 0, 0, tiled=True)  32.4 us
    reduce_scatter x1, waiting for transfers between devices, local(): partial = lax.psum_scatter(partial, 'tc', scatter_dimension=3, tiled=True)  19.7 us
    psum x1, blocking collectives, local(): lax.psum((jnp.sum(query_raw * query_raw, axis=-1), jnp.sum(key_raw * key_...  14.9 us
    all_gather x1, waiting for transfers between devices, local(): rows = lax.all_gather(received, 'tc', axis=2, tiled=True)  14.3 us
    all_to_all x1, starting transfers between devices, local(): returned = lax.all_to_all(back, ('req', 'th'), 0, 0, tiled=True)  12.8 us
  transfers between devices with their start and end apart: 5, of which 5 were waited for; matrix products, arithmetic and copies ran while one was open for 2% of the time, Pallas kernels for 0%

commit v1 on v0

--- a/solution.py
+++ b/solution.py
@@ -150,7 +150,9 @@
         "ict,tw->icw", select, normed_half, preferred_element_type=jnp.float32
     ).astype(jnp.bfloat16)
     received = lax.all_to_all(send_rows, "req", 0, 0, tiled=True)
-    rows = lax.all_gather(received, "tc", axis=2, tiled=True)
+    rows = jnp.concatenate(
+        lax.all_to_all(jnp.stack([received] * lax.axis_size("tc")), "tc", 0, 0), axis=2
+    )
     gate_up = jnp.einsum("scw,wgu->scgu", rows, w_gate_up[0], preferred_element_type=jnp.float32)
     activated = (jax.nn.silu(gate_up[..., 0, :]) * gate_up[..., 1, :]).astype(jnp.bfloat16)
     units_dev = w_down.shape[1]

time: 380 us -> 396 us (1.042)
  blocking collectives: 85.2 us -> 23.9 us
  waiting for transfers between devices: 182 us -> 223 us
  local copies, waits for them, and re-layouts: 52.8 us -> 75.5 us
  starting transfers between devices: 13.1 us -> 23.1 us
    all_to_all x1, blocking collectives: 70.3 us -> 9.06 us  [local(): lax.all_to_all(jnp.stack([received] * lax.axis_size('tc')), 'tc', 0, 0)]
    all_to_all x0 -> x1, waiting for transfers between devices: none -> 57.4 us  [local(): received = lax.all_to_all(send_rows, 'req', 0, 0, tiled=True)]
    reshape x0 -> x2, local copies, waits for them, and re-layouts: none -> 19.6 us  [local(): jnp.concatenate(lax.all_to_all(jnp.stack([received] * lax.axis_size('tc')...]
    all_gather x1 -> x0, waiting for transfers between devices: 14.3 us -> none  [local(): rows = lax.all_gather(received, 'tc', axis=2, tiled=True)]
    all_to_all x0 -> x1, starting transfers between devices: none -> 10.2 us  [local(): received = lax.all_to_all(send_rows, 'req', 0, 0, tiled=True)]
  transfers between devices with their start and end apart: 5 -> 5, of which waited for: 5 -> 5; matrix products, arithmetic and copies ran while one was open for 2% -> 1% of each run, Pallas kernels for 0% -> 0%
where the time goes in v1:
time: 396 us; the launch traced here: 395 us
  waiting for transfers between devices  223 us (56%)
  local copies, waits for them, and re-layouts  75.5 us (19%)
  matrix products  25.7 us (6%)
  blocking collectives  23.9 us (6%)
  starting transfers between devices  23.1 us (6%)
  between operations  14.3 us (4%)
  other arithmetic  8.73 us (2%)
    psum x1, waiting for transfers between devices, local(): residual = hidden.astype(jnp.float32) + lax.psum(attn_term, TP)  69.8 us
    all_to_all x1, waiting for transfers between devices, local(): received = lax.all_to_all(send_rows, 'req', 0, 0, tiled=True)  57.4 us
    reduce_scatter x1, waiting for transfers between devices, local(): partial = lax.psum_scatter(partial, 'tl', scatter_dimension=3, tiled=True)  46.5 us
    all_to_all x1, waiting for transfers between devices, local(): returned = lax.all_to_all(back, ('req', 'th'), 0, 0, tiled=True)  32.4 us
    reshape x2, local copies, waits for them, and re-layouts, local(): jnp.concatenate(lax.all_to_all(jnp.stack([received] * lax.axis_size('tc')...  19.6 us
    reduce_scatter x1, waiting for transfers between devices, local(): partial = lax.psum_scatter(partial, 'tc', scatter_dimension=3, tiled=True)  17.2 us
    psum x1, blocking collectives, local(): lax.psum((jnp.sum(query_raw * query_raw, axis=-1), jnp.sum(key_raw * key_...  14.8 us
    all_to_all x1, starting transfers between devices, local(): returned = lax.all_to_all(back, ('req', 'th'), 0, 0, tiled=True)  12.8 us
  transfers between devices with their start and end apart: 5, of which 5 were waited for; matrix products, arithmetic and copies ran while one was open for 1% of the time, Pallas kernels for 0%

profile of v1, /device:TPU:32, one launch (start us, length us, event | category | flops | bytes accessed | tf_op | source)
XLA Modules:
  0.0 394.6 jit_solution(8432448749137148182)
XLA Ops:
  7.3 4.9 %copy.89 = bf16[2048,3,256]{0,2,1:T(8,128)(2,1)} copy(bf16[2048,3,256]{2,0,1:T(8,128)(2,1)} %param.22) | data formatting | bytes 6291456 | tf_op args[7]
  12.2 0.3 fusion.11
  12.5 3.0 fusion.2
  15.6 0.8 slice.90
  16.4 0.4 convolution_minimum_fusion.6
  18.1 0.4 fusion.98
  18.8 14.8 %all-reduce = (f32[256]{0:T(256)S(1)}, f32[256]{0:T(256)S(1)}) all-reduce(f32[256]{0:T(256)S(1)} %get-tuple-element.3, f32[256]{0:T(256)S(1)} %get-tuple-element.2), channel_id=1, replica_groups=mesh['req'=32,'th'=2,'tl'=2,'tc'=2] {'th','tl','tc'}, use_global_device_ids=true, to_apply=%region_5.0 | all-reduce | flops 512 | bytes 4096 | tf_op jit(solution)/shard_map/psum | solution.py:85
  33.6 0.3 multiply_cosine_fusion
  34.9 0.8 copy.98
  35.8 0.8 copy.99
  36.6 0.6 broadcast_compare_fusion
  37.5 4.9 %gather_fusion = bf16[32,2,128,256]{3,2,1,0:T(8,128)(2,1)} fusion(bf16[2,32,128,256]{3,2,1,0:T(8,128)(2,1)} %param.16, s32[1024]{0:T(1024)S(1)} %pad_clamp_fusion.1), kind=kCustom, calls=%fused_computation | custom fusion | bytes 8388736 | tf_op jit(solution)/shard_map/gather | solution.py:94
  42.4 4.7 %fusion.96 = (bf16[1,32,128,256]{3,2,0,1:T(8,128)(2,1)}, bf16[1,32,128,256]{3,2,0,1:T(8,128)(2,1)}) fusion(bf16[2,32,128,256]{3,2,0,1:T(8,128)(2,1)} %bitcast.108), kind=kLoop, calls=%fused_computation.139 | loop fusion | bytes 8388608 | tf_op jit(solution)/shard_map/slice | solution.py:96
  47.1 2.5 reshape_squeeze.10
  49.7 4.0 %reshape_squeeze.9 = bf16[4,1024,2,128]{3,2,1,0:T(2,128)(2,1)} reshape(bf16[1,32,128,256]{3,2,0,1:T(8,128)(2,1)} %get-tuple-element.11) | data formatting | bytes 4194304 | tf_op jit(solution)/shard_map/reshape;squeeze | solution.py:97
  53.6 3.2 copy.91
  56.8 1.8 reshape.326
  58.6 1.7 copy.92
  60.4 1.0 fusion.99
  61.4 0.4 fusion.100
  61.8 0.5 fusion.18
  62.3 0.7 copy-done.4
  63.0 0.8 fusion.48
  64.0 1.8 fusion.70
  65.8 0.7 select_reduce_fusion
  66.9 69.8 %all-reduce.3.cloned.1.call-done = f32[256,2048]{1,0:T(8,128)} async-done(((f32[256,2048]{1,0:T(8,128)}), f32[256,2048]{1,0:T(8,128)}) %all-reduce.3.cloned.1.call-update) | async-done | bytes 2097168 | tf_op jit(solution)/shard_map/psum | solution.py:124
  136.7 1.9 multiply_reduce_fusion
  138.7 2.5 convolution_convert_fusion
  141.2 10.2 %all-to-all-start = ((bf16[32,40,1024]{2,1,0:T(8,128)(2,1)}), bf16[32,40,1024]{2,1,0:T(8,128)(2,1)}, u32[]{:S(2)}, u32[]{:S(2)}) async-start(bf16[32,40,1024]{2,1,0:T(8,128)(2,1)} %convolution_convert_fusion), calls=%async_computation | async-start | bytes 5242880 | tf_op jit(solution)/shard_map/all_to_all | solution.py:152
  151.5 1.6 reshape_squeeze.11
  153.1 57.4 %all-to-all-done = bf16[32,40,1024]{2,1,0:T(8,128)(2,1)} async-done(((bf16[32,40,1024]{2,1,0:T(8,128)(2,1)}), bf16[32,40,1024]{2,1,0:T(8,128)(2,1)}, u32[]{:S(2)}, u32[]{:S(2)}) %all-to-all-start) | async-done | bytes 2621472 | tf_op jit(solution)/shard_map/all_to_all | solution.py:152
  210.5 3.0 pad_maximum_fusion
  213.5 9.1 %all_to_all.15 = bf16[2,32,40,1024]{3,2,1,0:T(8,128)(2,1)} all-to-all(bf16[2,32,40,1024]{3,2,1,0:T(8,128)(2,1)S(1)} %pad_maximum_fusion), channel_id=1, replica_groups=mesh['req'=32,'th'=2,'tl'=2,'tc'=2] {'tc'}, dimensions={0} | all-to-all | bytes 10485760 | tf_op jit(solution)/shard_map/all_to_all | solution.py:154
  222.6 10.2 %copy.101 = bf16[32,40,2,1024]{3,2,1,0:T(2,128)(2,1)} copy(bf16[32,40,2,1024]{3,1,0,2:T(8,128)(2,1)} %bitcast.107) | data formatting | bytes 10485760 | tf_op jit(solution)/shard_map/reshape | solution.py:153
  232.7 9.4 %reshape.321 = bf16[32,40,2048,1]{2,1,0,3:T(8,128)(2,1)} reshape(bf16[32,40,2,1024]{3,2,1,0:T(2,128)(2,1)} %copy.101) | data formatting | bytes 10485760 | tf_op jit(solution)/shard_map/reshape | solution.py:153
  242.2 5.8 %fusion = f32[32,40,2,256]{3,1,2,0:T(8,128)S(1)} fusion(bf16[32,40,2048,1]{2,1,0,3:T(8,128)(2,1)} %reshape.321, bf16[2048,2,256]{2,1,0:T(2,128)(2,1)} %bitcast.120), kind=kOutput, calls=%fused_computation.4 | convolution fusion | flops 2684354560 | bytes 9961472 | tf_op jit(solution)/shard_map/scw,wgu->scgu/dot_general | solution.py:156
  247.9 4.0 %convert_bitcast_fusion = bf16[32,2,40,2,2,256]{5,2,3,4,1,0:T(8,128)(2,1)} fusion(bf16[256,2,2,2,256]{4,3,2,1,0:T(2,128)(2,1)S(1)} %copy-done.6, f32[32,40,2,256]{3,1,2,0:T(8,128)S(1)} %fusion), kind=kOutput, calls=%fused_computation.6 | convolution fusion | flops 1346764800 | bytes 8912896 | tf_op jit(solution)/shard_map/scu,uhlkd->shckld/dot_general | solution.py:160
  251.9 10.3 %copy.104 = bf16[32,2,40,2,2,256]{5,4,3,2,1,0:T(2,128)(2,1)} copy(bf16[32,2,40,2,2,256]{5,2,3,4,1,0:T(8,128)(2,1)} %convert_bitcast_fusion) | data formatting | bytes 10485760 | tf_op jit(solution)/shard_map/convert_element_type | solution.py:162
  262.3 9.3 %reshape.292 = bf16[32,2,40,1024]{3,2,1,0:T(8,128)(2,1)} reshape(bf16[32,2,40,2,2,256]{5,4,3,2,1,0:T(2,128)(2,1)} %copy.104) | data formatting | bytes 10485760 | tf_op jit(solution)/shard_map/reshape | solution.py:163
  271.7 17.2 %reduce-scatter.3.cloned.1.call-done = bf16[32,2,40,512]{3,2,1,0:T(8,128)(2,1)} async-done(((bf16[32,2,40,1024]{3,2,1,0:T(8,128)(2,1)}), bf16[32,2,40,512]{3,2,1,0:T(8,128)(2,1)}) %reduce-scatter.3.cloned.1.call-update) | async-done | bytes 2621456 | tf_op jit(solution)/shard_map/reduce_scatter | solution.py:164
  288.9 46.5 %reduce-scatter.5.cloned.1.call-done = bf16[32,2,40,256]{3,2,1,0:T(8,128)(2,1)} async-done(((bf16[32,2,40,512]{3,2,1,0:T(8,128)(2,1)}), bf16[32,2,40,256]{3,2,1,0:T(8,128)(2,1)}) %reduce-scatter.5.cloned.1.call-update) | async-done | bytes 1310736 | tf_op jit(solution)/shard_map/reduce_scatter | solution.py:165
  335.4 12.8 %all-to-all-start.2 = ((bf16[64,40,256]{2,1,0:T(8,128)(2,1)}), bf16[64,40,256]{2,1,0:T(8,128)(2,1)}, u32[]{:S(2)}, u32[]{:S(2)}) async-start(bf16[64,40,256]{2,1,0:T(8,128)(2,1)} %bitcast.109), calls=%async_computation.4 | async-start | bytes 2621440 | tf_op jit(solution)/shard_map/all_to_all | solution.py:167
  348.3 1.0 slice_bitcast_fusion
  349.4 0.6 gather_fusion.1
  350.0 0.6 gather_fusion.2
  350.7 0.6 pad_maximum_fusion.3
  351.3 32.4 %all-to-all-done.2 = bf16[64,40,256]{2,1,0:T(8,128)(2,1)} async-done(((bf16[64,40,256]{2,1,0:T(8,128)(2,1)}), bf16[64,40,256]{2,1,0:T(8,128)(2,1)}, u32[]{:S(2)}, u32[]{:S(2)}) %all-to-all-start.2) | async-done | bytes 1310752 | tf_op jit(solution)/shard_map/all_to_all | solution.py:167
  383.7 4.4 %fusion.40 = bf16[256,256]{1,0:T(8,128)(2,1)} fusion(bf16[64,40,256]{2,1,0:T(8,128)(2,1)} %all-to-all-done.2, f32[256,64]{0,1:T(8,128)S(1)} %copy-done.12, f32[256,64]{0,1:T(8,128)S(1)} %fusion.69, f32[256,2048]{1,0:T(8,128)S(1)} %get-tuple-element.9, s32[]{:T(128)S(6)} %select_n.47), kind=kOutput, calls=%fused_computation.48 | convolution fusion | flops 2014707712 | bytes 1835012 | tf_op jit(solution)/shard_map/dot_general | solution.py:169
  (92 shorter events, 3.9 us)
Async XLA Ops:
  7.2 56.8 %copy-start = (bf16[256,2048]{1,0:T(8,128)(2,1)S(1)}, bf16[256,2048]{1,0:T(8,128)(2,1)}, u32[]{:S(2)}) copy-start(bf16[256,2048]{1,0:T(8,128)(2,1)} %param.24) | copy-start | bytes 3145732
  7.2 129.5 %all-reduce.3.cloned.1.call-start = ((), (), s32[]{:S(2)}) async-start(), calls=%async_computation.5 | async-start | bytes 4194304 | tf_op jit(solution)/shard_map/psum | solution.py:124
  7.3 4.9 %copy-start.2 = (bf16[256,2048]{1,0:T(8,128)(2,1)S(1)}, bf16[256,2048]{1,0:T(8,128)(2,1)}, u32[]{:S(2)}) copy-start(bf16[256,2048]{1,0:T(8,128)(2,1)} %param.15) | copy-start | bytes 3145732
  7.3 5.2 %copy-start.20 = (f32[2048]{0:T(1024)S(1)}, f32[2048]{0:T(1024)}, u32[]{:S(2)}) copy-start(f32[2048]{0:T(1024)} %param.21) | copy-start | bytes 24580
  12.5 3.9 copy-start.17
  12.5 3.9 copy-start.19
  15.5 3.0 copy-start.7
  15.5 3.0 copy-start.15
  18.5 18.7 %copy-start.18 = (s32[4,8]{1,0:T(4,128)S(1)}, s32[4,8]{1,0:T(4,128)}, u32[]{:S(2)}) copy-start(s32[4,8]{1,0:T(4,128)} %param.20) | copy-start | bytes 388
  18.5 18.8 %copy-start.16 = (s32[4,8]{1,0:T(4,128)S(1)}, s32[4,8]{1,0:T(4,128)}, u32[]{:S(2)}) copy-start(s32[4,8]{1,0:T(4,128)} %param.17) | copy-start | bytes 388
  60.4 1.0 copy-start.8
  60.4 1.0 copy-start.9
  60.4 1.0 copy-start.11
  61.4 1.6 copy-start.4
  61.4 1.6 copy-start.10
  63.9 1.8 copy-start.13
  64.0 1.8 copy-start.14
  65.7 71.0 %copy-start.3 = (bf16[256,2048]{1,0:T(8,128)(2,1)S(1)}, bf16[256,2048]{1,0:T(8,128)(2,1)}, u32[]{:S(2)}) copy-start(bf16[256,2048]{1,0:T(8,128)(2,1)} %param.15) | copy-start | bytes 3145732
  66.9 71.7 %dynamic-slice-start = ((f32[2048]{0:T(1024)}, s32[]{:T(128)}), f32[1024]{0:T(1024)S(1)}, s32[]{:S(2)}) async-start(f32[2048]{0:T(1024)} %param.25, s32[]{:T(128)} %select_n.50), calls=%async_computation.8 | async-start | bytes 8704 | tf_op jit(solution)/shard_map/dynamic_slice | solution.py:148
  141.2 10.3 %copy-start.5 = (bf16[1,256,2048]{2,1,0:T(8,128)(2,1)S(1)}, bf16[1,256,2048]{2,1,0:T(8,128)(2,1)}, u32[]{:S(2)}) copy-start(bf16[1,256,2048]{2,1,0:T(8,128)(2,1)} %param.29) | copy-start | bytes 3145732
  141.2 69.3 %all-to-all-start = ((bf16[32,40,1024]{2,1,0:T(8,128)(2,1)}), bf16[32,40,1024]{2,1,0:T(8,128)(2,1)}, u32[]{:S(2)}, u32[]{:S(2)}) async-start(bf16[32,40,1024]{2,1,0:T(8,128)(2,1)} %convolution_convert_fusion), calls=%async_computation | async-start | bytes 5242880 | tf_op jit(solution)/shard_map/all_to_all | solution.py:152
  151.4 137.4 %reduce-scatter.3.cloned.1.call-start = ((), (), s32[]{:S(2)}) async-start(), calls=%async_computation.6 | async-start | bytes 7864320 | tf_op jit(solution)/shard_map/reduce_scatter | solution.py:164
  242.2 5.8 %copy-start.6 = (bf16[256,2,2,2,256]{4,3,2,1,0:T(2,128)(2,1)S(1)}, bf16[256,2,2,2,256]{4,3,2,1,0:T(2,128)(2,1)}, u32[]{:S(2)}) copy-start(bf16[256,2,2,2,256]{4,3,2,1,0:T(2,128)(2,1)} %reshape_squeeze.11) | copy-start | bytes 3145732
  271.6 63.8 %reduce-scatter.5.cloned.1.call-start = ((), (), s32[]{:S(2)}) async-start(), calls=%async_computation.7 | async-start | bytes 3932160 | tf_op jit(solution)/shard_map/reduce_scatter | solution.py:165
  288.9 94.9 %copy-start.12 = (f32[256,64]{0,1:T(8,128)S(1)}, f32[256,64]{0,1:T(8,128)}, u32[]{:S(2)}) copy-start(f32[256,64]{0,1:T(8,128)} %get-tuple-element.4) | copy-start | bytes 196612
  335.4 48.3 %all-to-all-start.2 = ((bf16[64,40,256]{2,1,0:T(8,128)(2,1)}), bf16[64,40,256]{2,1,0:T(8,128)(2,1)}, u32[]{:S(2)}, u32[]{:S(2)}) async-start(bf16[64,40,256]{2,1,0:T(8,128)(2,1)} %bitcast.109), calls=%async_computation.4 | async-start | bytes 2621440 | tf_op jit(solution)/shard_map/all_to_all | solution.py:167
  383.7 4.4 %copy-start.1 = (bf16[256,2048]{1,0:T(8,128)(2,1)S(1)}, bf16[256,2048]{1,0:T(8,128)(2,1)}, u32[]{:S(2)}) copy-start(bf16[256,2048]{1,0:T(8,128)(2,1)} %param.24) | copy-start | bytes 3145732
Sparse Core Ops, SparseCore 0:
  65.9 70.7 all-reduce.2
  271.7 17.0 reduce-scatter.2
  291.3 44.0 reduce-scatter.4
